TPU v7x, 32 devices: a whole 2x2x4 slice. The times are simulated.
32 devices in a mesh: wave: 4 (over y, core), lev: 4 (over z), cpl: 2 (over x).
Axes of the slice: x: 2, y: 2, z: 4, core: 2. Of those that a mesh axis runs over, the one named last changes fastest.
Arguments:
- spectral: bfloat16 [1280, 2, 4, 24, 1280], P('wave', None, None, 'lev'), may hold values from -0.125 to 0.125
- legendre: bfloat16 [1280, 16, 1280], P('wave', 'cpl'), may hold values from -0.15625 to 0.15625
- wavenumber: int32 [1280], replicated, may hold values from 0 to 1279, each once
- level_weight: float32 [24], P('lev'), may hold values from 0.1 to 1
- source_row: int32 [16], replicated, may hold values from 0 to 14
- row_weight: float32 [16], replicated, may hold values from 0.2 to 0.8
Outputs:
- ocean_flux: float32 [16, 4, 4320], P(('wave', 'cpl'), None, 'lev')
All inputs are finite; a program needn't handle non-finite values.
Results may differ from a plain program's by a relative error of at most 0.0041.
Values may be sent and summed in bfloat16 or wider, within the bound.
No kernel may reach another device: no remote copies, remote signals or barrier semaphores. Data moves between devices by JAX's collectives and lax.ppermute only.
A program may use at most 192 MiB of HBM per device.

v0:
```python
import math
import jax
import jax.numpy as jnp
from jax import lax
from jax.sharding import PartitionSpec as P

NLON = 4320


def phase_angle(phase, lon_total):
    return phase.astype(jnp.float32) * (2.0 * math.pi / lon_total)


def surface_flux(grid_vals, level_weight):
    wind_speed = jnp.sqrt(grid_vals[..., 0, :, :] ** 2 + grid_vals[..., 1, :, :] ** 2 + 0.25)
    return jnp.sum(level_weight[:, None] * wind_speed[..., None, :, :] * grid_vals, axis=-2)


def latitude_order(gathered, wave_count, cpl_count, lat_dev):
    trailing = gathered.shape[1:]
    gathered = gathered.reshape((wave_count, cpl_count, lat_dev) + trailing)
    gathered = jnp.swapaxes(gathered, 0, 1)
    return gathered.reshape((wave_count * cpl_count * lat_dev,) + trailing)


def interpolate(gathered, source, weight_hi):
    lower = jnp.take(gathered, source, axis=0)
    upper = jnp.take(gathered, source + 1, axis=0)
    return (1.0 - weight_hi[:, None, None]) * lower + weight_hi[:, None, None] * upper


def local(spectral, legendre, wavenumber, level_weight, source_row, row_weight):
    slot_count = spectral.shape[0]
    fields = spectral.shape[2]
    levels = spectral.shape[3]
    degree = spectral.shape[4]
    channels = 2 * fields * levels
    wave_count = lax.axis_size("wave")
    cpl_count = lax.axis_size("cpl")
    wave_at = lax.axis_index("wave")
    cpl_at = lax.axis_index("cpl")
    owned_waves = lax.dynamic_slice_in_dim(wavenumber, wave_at * slot_count, slot_count)
    coefficient = spectral.reshape(slot_count, channels, degree)
    in_triangle = (
        lax.broadcasted_iota(jnp.int32, (slot_count, 1, degree), 2)
        < (degree - owned_waves)[:, None, None]
    )
    coefficient = jnp.where(in_triangle, coefficient, jnp.zeros_like(coefficient))
    spec_grid = jnp.einsum(
        "skj,slj->slk", coefficient, legendre, preferred_element_type=jnp.float32
    ).astype(jnp.bfloat16)
    by_latitude = lax.all_to_all(spec_grid, "wave", split_axis=1, concat_axis=0, tiled=True)
    total_slots = by_latitude.shape[0]
    lat_dev = by_latitude.shape[1]
    rows_in = (
        by_latitude.reshape(total_slots, lat_dev, 2, fields * levels)
        .transpose(1, 3, 0, 2)
        .reshape(lat_dev * fields * levels, 2 * total_slots)
    )
    lon_block = NLON // 8
    factor = jnp.where(wavenumber == 0, 1.0, 2.0).astype(jnp.float32)[:, None]
    offsets = jnp.arange(lon_block, dtype=jnp.int32)
    base_angle = phase_angle(wavenumber[:, None] * offsets[None, :] % NLON, NLON)
    base_cos = jnp.cos(base_angle)
    base_sin = jnp.sin(base_angle)

    def one_block(first_lon):
        start_angle = phase_angle(wavenumber * first_lon % NLON, NLON)[:, None]
        start_cos = jnp.cos(start_angle)
        start_sin = jnp.sin(start_angle)
        cos_vals = start_cos * base_cos - start_sin * base_sin
        sin_vals = start_sin * base_cos + start_cos * base_sin
        fourier = (
            jnp.stack([factor * cos_vals, -factor * sin_vals], axis=1)
            .astype(jnp.bfloat16)
            .reshape(2 * total_slots, lon_block)
        )
        grid_vals = jnp.dot(rows_in, fourier, preferred_element_type=jnp.float32).reshape(
            lat_dev, fields, levels, lon_block
        )
        return surface_flux(grid_vals, level_weight)

    block_starts = jnp.arange(8, dtype=jnp.int32) * lon_block
    per_block = lax.map(one_block, block_starts)
    partial_value = per_block.transpose(1, 2, 0, 3).reshape(lat_dev, fields, NLON)
    own_first = (wave_at * cpl_count + cpl_at) * lat_dev
    source = lax.dynamic_slice_in_dim(source_row, own_first, lat_dev)
    weight_hi = lax.dynamic_slice_in_dim(row_weight, own_first, lat_dev)
    strip_width = NLON // lax.axis_size("lev")
    summed = lax.psum(partial_value, "lev")
    gathered = lax.all_gather(summed, ("wave", "cpl"), axis=0, tiled=True)
    gathered = latitude_order(gathered, wave_count, cpl_count, lat_dev)
    gathered = lax.dynamic_slice_in_dim(
        gathered, lax.axis_index("lev") * strip_width, strip_width, 2
    )
    return interpolate(gathered, source, weight_hi)


def solution(mesh):
    placed = (P("wave", None, None, "lev", None), P("wave", "cpl", None), P(), P("lev"), P(), P())
    return jax.shard_map(
        local,
        mesh=mesh,
        in_specs=placed,
        out_specs=P(("wave", "cpl"), None, "lev"),
        check_vma=False,
    )
```

profile of v0, /device:TPU:0, one launch (start us, length us, event | category | flops | bytes accessed | tf_op | source)
XLA Modules:
  0.0 437.1 jit_solution(12876540771261802303)
XLA Ops:
  6.5 0.8 dynamic-slice_subtract_fusion
  7.6 26.6 %copy.16 = bf16[320,2,4,6,1280]{4,0,3,2,1:T(8,128)(2,1)} copy(bf16[320,2,4,6,1280]{4,2,3,1,0:T(4,128)(2,1)} %param.10) | data formatting | bytes 78643200 | tf_op args[0]
  34.2 26.6 %bitcast_select_fusion = bf16[320,48,1280]{2,0,1:T(8,128)(2,1)} fusion(bf16[320,2,4,6,1280]{4,0,3,2,1:T(8,128)(2,1)} %copy.16, pred[320,1280]{1,0:T(8,128)(4,1)S(1)} %iota_compare_fusion), kind=kLoop, calls=%fused_computation.40 | loop fusion | flops 19660800 | bytes 79052800 | tf_op jit(solution)/shard_map/jit(_where)/select_n | solution.py:48
  60.8 47.0 %fusion.31 = bf16[320,8,48]{2,1,0:T(8,128)(2,1)S(1)} fusion(bf16[320,8,1280]{2,1,0:T(8,128)(2,1)} %param.11, bf16[320,48,1280]{2,0,1:T(8,128)(2,1)} %bitcast_select_fusion), kind=kOutput, calls=%fused_computation.45 | convolution fusion | flops 314695680 | bytes 46120960 | tf_op jit(solution)/shard_map/skj,slj->slk/dot_general | solution.py:49
  107.8 1.1 copy.18
  109.0 4.2 all-to-all-start
  113.3 6.3 %all-to-all-done = bf16[320,8,48]{0,2,1:T(8,128)(2,1)S(1)} async-done(((bf16[320,8,48]{0,2,1:T(8,128)(2,1)}), bf16[320,8,48]{0,2,1:T(8,128)(2,1)S(1)}, u32[]{:S(2)}, u32[]{:S(2)}) %all-to-all-start) | async-done | bytes 245792 | tf_op jit(solution)/shard_map/all_to_all | solution.py:52
  120.0 1.7 copy.20
  121.7 0.6 reshape.276
  122.4 0.9 copy.21
  123.3 240.5 %while.14 = (s32[]{:T(128)}, f32[8,2,4,540]{3,2,1,0:T(4,128)}, f32[6]{0:T(128)S(1)}, f32[1280,1]{0,1:T(1,128)S(1)}, s32[8]{0:T(128)S(1)}, /*index=5*/s32[1280]{0...) while((s32[]{:T(128)}, f32[8,2,4,540]{3,2,1,0:T(4,128)}, ...), condition=%wide.region_2.3_spmd.clone.clone, body=%wide.region_0.2_spmd.clone.clone.sunk | while | flops 147317040 | bytes 22999700 | solution.py:84
  123.9 0.6 fusion.46
  124.5 12.4 %fusion.47 = (bf16[1280,1,540]{0,2,1:T(8,128)(2,1)S(1)}, bf16[1280,1,540]{0,2,1:T(8,128)(2,1)S(1)}) fusion(s32[1280]{0:T(1024)S(1)} %get-tuple-element.302, f32[1280]{0:T(1024)S(1)} %get-tuple-element.273, f32[1280]{0:T(1024)S(1)} %get-tuple-element.274, f32[1280]{0:T(1024)S(1)} %reduce.4, f32[1280]{0:T(1024)S(1)} %reduce.5), kind=kLoop, calls=%fused_computation.12.clone.1 | loop fusion | flops 13132800 | bytes 2790400 | tf_op jit(solution)/shard_map/convert
  137.2 7.2 %copy.33 = bf16[1280,2,540]{2,1,0:T(2,128)(2,1)} copy(bf16[1280,2,540]{0,2,1:T(8,128)(2,1)S(1)} %pad_maximum_fusion.2) | data formatting | bytes 5529600 | tf_op jit(solution)/shard_map/while/body/eval_jaxpr/stack | solution.py:74
  144.4 6.6 %convert_element_type.80 = bf16[2560,540]{1,0:T(8,128)(2,1)S(1)} reshape(bf16[1280,2,540]{2,1,0:T(2,128)(2,1)} %copy.33) | data formatting | bytes 5529600 | tf_op jit(solution)/shard_map/while/body/eval_jaxpr/convert_element_type | solution.py:75
  151.0 1.5 convolution_bitcast_fusion.2
  152.7 0.6 bitcast_dynamic-update-slice_fusion.2
  153.9 0.6 fusion.46
  154.6 12.4 %fusion.47 = (bf16[1280,1,540]{0,2,1:T(8,128)(2,1)S(1)}, bf16[1280,1,540]{0,2,1:T(8,128)(2,1)S(1)}) fusion(s32[1280]{0:T(1024)S(1)} %get-tuple-element.302, f32[1280]{0:T(1024)S(1)} %get-tuple-element.273, f32[1280]{0:T(1024)S(1)} %get-tuple-element.274, f32[1280]{0:T(1024)S(1)} %reduce.4, f32[1280]{0:T(1024)S(1)} %reduce.5), kind=kLoop, calls=%fused_computation.12.clone.1 | loop fusion | flops 13132800 | bytes 2790400 | tf_op jit(solution)/shard_map/convert
  167.3 7.2 %copy.33 = bf16[1280,2,540]{2,1,0:T(2,128)(2,1)} copy(bf16[1280,2,540]{0,2,1:T(8,128)(2,1)S(1)} %pad_maximum_fusion.2) | data formatting | bytes 5529600 | tf_op jit(solution)/shard_map/while/body/eval_jaxpr/stack | solution.py:74
  174.5 6.6 %convert_element_type.80 = bf16[2560,540]{1,0:T(8,128)(2,1)S(1)} reshape(bf16[1280,2,540]{2,1,0:T(2,128)(2,1)} %copy.33) | data formatting | bytes 5529600 | tf_op jit(solution)/shard_map/while/body/eval_jaxpr/convert_element_type | solution.py:75
  181.1 1.5 convolution_bitcast_fusion.2
  182.8 0.6 bitcast_dynamic-update-slice_fusion.2
  184.0 0.6 fusion.46
  184.7 12.4 %fusion.47 = (bf16[1280,1,540]{0,2,1:T(8,128)(2,1)S(1)}, bf16[1280,1,540]{0,2,1:T(8,128)(2,1)S(1)}) fusion(s32[1280]{0:T(1024)S(1)} %get-tuple-element.302, f32[1280]{0:T(1024)S(1)} %get-tuple-element.273, f32[1280]{0:T(1024)S(1)} %get-tuple-element.274, f32[1280]{0:T(1024)S(1)} %reduce.4, f32[1280]{0:T(1024)S(1)} %reduce.5), kind=kLoop, calls=%fused_computation.12.clone.1 | loop fusion | flops 13132800 | bytes 2790400 | tf_op jit(solution)/shard_map/convert
  197.3 7.2 %copy.33 = bf16[1280,2,540]{2,1,0:T(2,128)(2,1)} copy(bf16[1280,2,540]{0,2,1:T(8,128)(2,1)S(1)} %pad_maximum_fusion.2) | data formatting | bytes 5529600 | tf_op jit(solution)/shard_map/while/body/eval_jaxpr/stack | solution.py:74
  204.5 6.6 %convert_element_type.80 = bf16[2560,540]{1,0:T(8,128)(2,1)S(1)} reshape(bf16[1280,2,540]{2,1,0:T(2,128)(2,1)} %copy.33) | data formatting | bytes 5529600 | tf_op jit(solution)/shard_map/while/body/eval_jaxpr/convert_element_type | solution.py:75
  211.2 1.5 convolution_bitcast_fusion.2
  212.9 0.6 bitcast_dynamic-update-slice_fusion.2
  214.0 0.6 fusion.46
  214.7 12.4 %fusion.47 = (bf16[1280,1,540]{0,2,1:T(8,128)(2,1)S(1)}, bf16[1280,1,540]{0,2,1:T(8,128)(2,1)S(1)}) fusion(s32[1280]{0:T(1024)S(1)} %get-tuple-element.302, f32[1280]{0:T(1024)S(1)} %get-tuple-element.273, f32[1280]{0:T(1024)S(1)} %get-tuple-element.274, f32[1280]{0:T(1024)S(1)} %reduce.4, f32[1280]{0:T(1024)S(1)} %reduce.5), kind=kLoop, calls=%fused_computation.12.clone.1 | loop fusion | flops 13132800 | bytes 2790400 | tf_op jit(solution)/shard_map/convert
  227.4 7.2 %copy.33 = bf16[1280,2,540]{2,1,0:T(2,128)(2,1)} copy(bf16[1280,2,540]{0,2,1:T(8,128)(2,1)S(1)} %pad_maximum_fusion.2) | data formatting | bytes 5529600 | tf_op jit(solution)/shard_map/while/body/eval_jaxpr/stack | solution.py:74
  234.6 6.6 %convert_element_type.80 = bf16[2560,540]{1,0:T(8,128)(2,1)S(1)} reshape(bf16[1280,2,540]{2,1,0:T(2,128)(2,1)} %copy.33) | data formatting | bytes 5529600 | tf_op jit(solution)/shard_map/while/body/eval_jaxpr/convert_element_type | solution.py:75
  241.2 1.5 convolution_bitcast_fusion.2
  242.9 0.6 bitcast_dynamic-update-slice_fusion.2
  244.1 0.6 fusion.46
  244.8 12.4 %fusion.47 = (bf16[1280,1,540]{0,2,1:T(8,128)(2,1)S(1)}, bf16[1280,1,540]{0,2,1:T(8,128)(2,1)S(1)}) fusion(s32[1280]{0:T(1024)S(1)} %get-tuple-element.302, f32[1280]{0:T(1024)S(1)} %get-tuple-element.273, f32[1280]{0:T(1024)S(1)} %get-tuple-element.274, f32[1280]{0:T(1024)S(1)} %reduce.4, f32[1280]{0:T(1024)S(1)} %reduce.5), kind=kLoop, calls=%fused_computation.12.clone.1 | loop fusion | flops 13132800 | bytes 2790400 | tf_op jit(solution)/shard_map/convert
  257.5 7.2 %copy.33 = bf16[1280,2,540]{2,1,0:T(2,128)(2,1)} copy(bf16[1280,2,540]{0,2,1:T(8,128)(2,1)S(1)} %pad_maximum_fusion.2) | data formatting | bytes 5529600 | tf_op jit(solution)/shard_map/while/body/eval_jaxpr/stack | solution.py:74
  264.7 6.6 %convert_element_type.80 = bf16[2560,540]{1,0:T(8,128)(2,1)S(1)} reshape(bf16[1280,2,540]{2,1,0:T(2,128)(2,1)} %copy.33) | data formatting | bytes 5529600 | tf_op jit(solution)/shard_map/while/body/eval_jaxpr/convert_element_type | solution.py:75
  271.3 1.5 convolution_bitcast_fusion.2
  273.0 0.6 bitcast_dynamic-update-slice_fusion.2
  274.2 0.6 fusion.46
  274.9 12.4 %fusion.47 = (bf16[1280,1,540]{0,2,1:T(8,128)(2,1)S(1)}, bf16[1280,1,540]{0,2,1:T(8,128)(2,1)S(1)}) fusion(s32[1280]{0:T(1024)S(1)} %get-tuple-element.302, f32[1280]{0:T(1024)S(1)} %get-tuple-element.273, f32[1280]{0:T(1024)S(1)} %get-tuple-element.274, f32[1280]{0:T(1024)S(1)} %reduce.4, f32[1280]{0:T(1024)S(1)} %reduce.5), kind=kLoop, calls=%fused_computation.12.clone.1 | loop fusion | flops 13132800 | bytes 2790400 | tf_op jit(solution)/shard_map/convert
  287.5 7.2 %copy.33 = bf16[1280,2,540]{2,1,0:T(2,128)(2,1)} copy(bf16[1280,2,540]{0,2,1:T(8,128)(2,1)S(1)} %pad_maximum_fusion.2) | data formatting | bytes 5529600 | tf_op jit(solution)/shard_map/while/body/eval_jaxpr/stack | solution.py:74
  294.7 6.6 %convert_element_type.80 = bf16[2560,540]{1,0:T(8,128)(2,1)S(1)} reshape(bf16[1280,2,540]{2,1,0:T(2,128)(2,1)} %copy.33) | data formatting | bytes 5529600 | tf_op jit(solution)/shard_map/while/body/eval_jaxpr/convert_element_type | solution.py:75
  301.3 1.5 convolution_bitcast_fusion.2
  303.1 0.6 bitcast_dynamic-update-slice_fusion.2
  304.2 0.6 fusion.46
  304.9 12.4 %fusion.47 = (bf16[1280,1,540]{0,2,1:T(8,128)(2,1)S(1)}, bf16[1280,1,540]{0,2,1:T(8,128)(2,1)S(1)}) fusion(s32[1280]{0:T(1024)S(1)} %get-tuple-element.302, f32[1280]{0:T(1024)S(1)} %get-tuple-element.273, f32[1280]{0:T(1024)S(1)} %get-tuple-element.274, f32[1280]{0:T(1024)S(1)} %reduce.4, f32[1280]{0:T(1024)S(1)} %reduce.5), kind=kLoop, calls=%fused_computation.12.clone.1 | loop fusion | flops 13132800 | bytes 2790400 | tf_op jit(solution)/shard_map/convert
  317.6 7.2 %copy.33 = bf16[1280,2,540]{2,1,0:T(2,128)(2,1)} copy(bf16[1280,2,540]{0,2,1:T(8,128)(2,1)S(1)} %pad_maximum_fusion.2) | data formatting | bytes 5529600 | tf_op jit(solution)/shard_map/while/body/eval_jaxpr/stack | solution.py:74
  324.8 6.6 %convert_element_type.80 = bf16[2560,540]{1,0:T(8,128)(2,1)S(1)} reshape(bf16[1280,2,540]{2,1,0:T(2,128)(2,1)} %copy.33) | data formatting | bytes 5529600 | tf_op jit(solution)/shard_map/while/body/eval_jaxpr/convert_element_type | solution.py:75
  331.4 1.5 convolution_bitcast_fusion.2
  334.3 0.6 fusion.46
  335.0 12.4 %fusion.47 = (bf16[1280,1,540]{0,2,1:T(8,128)(2,1)S(1)}, bf16[1280,1,540]{0,2,1:T(8,128)(2,1)S(1)}) fusion(s32[1280]{0:T(1024)S(1)} %get-tuple-element.302, f32[1280]{0:T(1024)S(1)} %get-tuple-element.273, f32[1280]{0:T(1024)S(1)} %get-tuple-element.274, f32[1280]{0:T(1024)S(1)} %reduce.4, f32[1280]{0:T(1024)S(1)} %reduce.5), kind=kLoop, calls=%fused_computation.12.clone.1 | loop fusion | flops 13132800 | bytes 2790400 | tf_op jit(solution)/shard_map/convert
  347.7 7.2 %copy.33 = bf16[1280,2,540]{2,1,0:T(2,128)(2,1)} copy(bf16[1280,2,540]{0,2,1:T(8,128)(2,1)S(1)} %pad_maximum_fusion.2) | data formatting | bytes 5529600 | tf_op jit(solution)/shard_map/while/body/eval_jaxpr/stack | solution.py:74
  354.9 6.6 %convert_element_type.80 = bf16[2560,540]{1,0:T(8,128)(2,1)S(1)} reshape(bf16[1280,2,540]{2,1,0:T(2,128)(2,1)} %copy.33) | data formatting | bytes 5529600 | tf_op jit(solution)/shard_map/while/body/eval_jaxpr/convert_element_type | solution.py:75
  361.5 1.5 convolution_bitcast_fusion.2
  363.2 0.6 bitcast_dynamic-update-slice_fusion.2
  363.8 0.9 copy.22
  364.8 0.8 reshape.277
  365.6 35.4 %all-reduce.2.cloned.1.call-done = f32[2,4,4320]{2,1,0:T(4,128)} async-done(((f32[2,4,4320]{2,1,0:T(4,128)}), f32[2,4,4320]{2,1,0:T(4,128)}) %all-reduce.2.cloned.1.call-update) | async-done | bytes 138256 | tf_op jit(solution)/shard_map/psum | solution.py:90
  401.2 25.6 %all-gather.2.cloned.1.call-done = f32[16,4,4320]{2,1,0:T(4,128)} async-done(((f32[2,4,4320]{2,1,0:T(4,128)}), f32[16,4,4320]{2,1,0:T(4,128)}) %all-gather.2.cloned.1.call-update) | async-done | bytes 1105936 | tf_op jit(solution)/shard_map/all_gather | solution.py:91
  426.9 1.3 copy.23
  429.6 0.7 fusion.34
  (83 shorter events, 11.2 us)
Async XLA Ops:
  60.8 52.4 %copy-start = (s32[1280]{0:T(1024)S(1)}, s32[1280]{0:T(1024)}, u32[]{:S(2)}) copy-start(s32[1280]{0:T(1024)} %param.12) | copy-start | bytes 15364
  109.0 10.6 %all-to-all-start = ((bf16[320,8,48]{0,2,1:T(8,128)(2,1)}), bf16[320,8,48]{0,2,1:T(8,128)(2,1)S(1)}, u32[]{:S(2)}, u32[]{:S(2)}) async-start(bf16[320,8,48]{0,2,1:T(8,128)(2,1)} %copy.18), calls=%async_computation | async-start | bytes 589824 | tf_op jit(solution)/shard_map/all_to_all | solution.py:52
  113.2 287.8 %all-reduce.2.cloned.1.call-start = ((), (), s32[]{:S(2)}) async-start(), calls=%async_computation.1 | async-start | bytes 278528 | tf_op jit(solution)/shard_map/psum | solution.py:90
  113.2 10.0 %copy-start.1 = (f32[6]{0:T(128)S(1)}, f32[6]{0:T(128)}, u32[]{:S(2)}) copy-start(f32[6]{0:T(128)} %param.13) | copy-start | bytes 76
  123.3 277.8 %copy-start.2 = (f32[16]{0:T(128)S(1)}, f32[16]{0:T(128)}, u32[]{:S(2)}) copy-start(f32[16]{0:T(128)} %param.15) | copy-start | bytes 196
  123.3 277.9 %copy-start.3 = (s32[16]{0:T(128)S(1)}, s32[16]{0:T(128)}, u32[]{:S(2)}) copy-start(s32[16]{0:T(128)} %param.14) | copy-start | bytes 196
  365.6 61.3 %all-gather.2.cloned.1.call-start = ((), (), s32[]{:S(2)}) async-start(), calls=%async_computation.2 | async-start | bytes 1253376 | tf_op jit(solution)/shard_map/all_gather | solution.py:91
Sparse Core Ops, SparseCore 0:
  365.7 35.2 all-reduce.1
  403.0 23.7 all-gather.1
where the time goes:
time: 439 us; the launch traced here: 437 us
  local copies, waits for them, and re-layouts  156 us (36%)
  other arithmetic  136 us (31%)
  waiting for transfers between devices  67.4 us (15%)
  matrix products  59.3 us (14%)
  between operations  13.5 us (3%)
    another operation x24, other arithmetic  99.7 us
    another operation x8, local copies, waits for them, and re-layouts, one_block(): jnp.stack([factor * cos_vals, -factor * sin_vals], axis=1)  57.6 us
    convert_element_type x8, local copies, waits for them, and re-layouts, one_block(): fourier = jnp.stack([factor * cos_vals, -factor * sin_vals], axis=1).asty...  52.9 us
    dot_general x1, matrix products, local(): jnp.einsum('skj,slj->slk', coefficient, legendre, preferred_element_type=...  47 us
    psum x1, waiting for transfers between devices, local(): summed = lax.psum(partial_value, 'lev')  35.4 us
    unnamed x10, local copies, waits for them, and re-layouts  27.6 us
    select_n x1, other arithmetic, local(): jnp.where(in_triangle, coefficient, jnp.zeros_like(coefficient))  26.6 us
    all_gather x1, waiting for transfers between devices, local(): gathered = lax.all_gather(summed, ('wave', 'cpl'), axis=0, tiled=True)  25.6 us
  transfers between devices with their start and end apart: 3, of which 3 were waited for; matrix products, arithmetic and copies ran while one was open for 0% of the time, Pallas kernels for 0%

commit v1 on v0

--- a/solution.py
+++ b/solution.py
@@ -88,7 +88,22 @@
     weight_hi = lax.dynamic_slice_in_dim(row_weight, own_first, lat_dev)
     strip_width = NLON // lax.axis_size("lev")
     summed = lax.psum(partial_value, "lev")
-    gathered = lax.all_gather(summed, ("wave", "cpl"), axis=0, tiled=True)
+    ways, here, step = (
+        lax.axis_size(("wave", "cpl")),
+        lax.axis_index(("wave", "cpl")),
+        summed.shape[0],
+    )
+    line, have = (summed, 1)
+    while have < ways:
+        line = jnp.concatenate(
+            [
+                line,
+                lax.ppermute(line, ("wave", "cpl"), [(d, (d - have) % ways) for d in range(ways)]),
+            ],
+            axis=0,
+        )
+        have = 2 * have
+    gathered = jnp.roll(line, here * step, axis=0)
     gathered = latitude_order(gathered, wave_count, cpl_count, lat_dev)
     gathered = lax.dynamic_slice_in_dim(
         gathered, lax.axis_index("lev") * strip_width, strip_width, 2

time: 439 us -> 441 us (level)
    all_gather x1 -> x0, waiting for transfers between devices: 25.6 us -> none  [local(): gathered = lax.all_gather(summed, ('wave', 'cpl'), axis=0, tiled=True)]
    ppermute x0 -> x3, waiting for transfers between devices: none -> 22.3 us  [local(): lax.ppermute(line, ('wave', 'cpl'), [(d, (d - have) % ways) for d in rang...]
    unnamed x10 -> x19, local copies, waits for them, and re-layouts: 27.6 us -> 28.8 us
  transfers between devices with their start and end apart: 3 -> 5, of which waited for: 3 -> 5; matrix products, arithmetic and copies ran while one was open for 0% -> 0% of each run, Pallas kernels for 0% -> 0%
where the time goes in v1:
time: 441 us; the launch traced here: 439 us
  local copies, waits for them, and re-layouts  157 us (36%)
  other arithmetic  139 us (32%)
  waiting for transfers between devices  63.9 us (14%)
  matrix products  59.3 us (13%)
  between operations  13.6 us (3%)
  starting transfers between devices  5.84 us (1%)
    another operation x24, other arithmetic  99.7 us
    another operation x8, local copies, waits for them, and re-layouts, one_block(): jnp.stack([factor * cos_vals, -factor * sin_vals], axis=1)  58 us
    convert_element_type x8, local copies, waits for them, and re-layouts, one_block(): fourier = jnp.stack([factor * cos_vals, -factor * sin_vals], axis=1).asty...  52.9 us
    dot_general x1, matrix products, local(): jnp.einsum('skj,slj->slk', coefficient, legendre, preferred_element_type=...  47 us
    psum x1, waiting for transfers between devices, local(): summed = lax.psum(partial_value, 'lev')  35.3 us
    unnamed x19, local copies, waits for them, and re-layouts  28.8 us
    select_n x1, other arithmetic, local(): jnp.where(in_triangle, coefficient, jnp.zeros_like(coefficient))  26.6 us
    ppermute x3, waiting for transfers between devices, local(): lax.ppermute(line, ('wave', 'cpl'), [(d, (d - have) % ways) for d in rang...  22.3 us
  transfers between devices with their start and end apart: 5, of which 5 were waited for; matrix products, arithmetic and copies ran while one was open for 0% of the time, Pallas kernels for 0%

profile of v1, /device:TPU:0, one launch (start us, length us, event | category | flops | bytes accessed | tf_op | source)
XLA Modules:
  0.0 439.5 jit_solution(14991474685655498898)
XLA Ops:
  6.5 0.8 dynamic-slice_subtract_fusion
  7.6 26.6 %copy.23 = bf16[320,2,4,6,1280]{4,0,3,2,1:T(8,128)(2,1)} copy(bf16[320,2,4,6,1280]{4,2,3,1,0:T(4,128)(2,1)} %param.10) | data formatting | bytes 78643200 | tf_op args[0]
  34.3 26.6 %bitcast_select_fusion = bf16[320,48,1280]{2,0,1:T(8,128)(2,1)} fusion(bf16[320,2,4,6,1280]{4,0,3,2,1:T(8,128)(2,1)} %copy.23, pred[320,1280]{1,0:T(8,128)(4,1)S(1)} %iota_compare_fusion), kind=kLoop, calls=%fused_computation.40 | loop fusion | flops 19660800 | bytes 79052800 | tf_op jit(solution)/shard_map/jit(_where)/select_n | solution.py:48
  60.9 47.0 %fusion.31 = bf16[320,8,48]{2,1,0:T(8,128)(2,1)S(1)} fusion(bf16[320,8,1280]{2,1,0:T(8,128)(2,1)} %param.11, bf16[320,48,1280]{2,0,1:T(8,128)(2,1)} %bitcast_select_fusion), kind=kOutput, calls=%fused_computation.45 | convolution fusion | flops 314695680 | bytes 46120960 | tf_op jit(solution)/shard_map/skj,slj->slk/dot_general | solution.py:49
  107.9 1.1 copy.25
  109.0 4.2 all-to-all-start
  113.4 6.2 %all-to-all-done = bf16[320,8,48]{0,2,1:T(8,128)(2,1)S(1)} async-done(((bf16[320,8,48]{0,2,1:T(8,128)(2,1)}), bf16[320,8,48]{0,2,1:T(8,128)(2,1)S(1)}, u32[]{:S(2)}, u32[]{:S(2)}) %all-to-all-start) | async-done | bytes 245792 | tf_op jit(solution)/shard_map/all_to_all | solution.py:52
  120.1 1.7 copy.27
  122.4 0.9 copy.28
  123.3 242.5 %while.14 = (s32[]{:T(128)}, f32[8,2,4,540]{3,2,1,0:T(4,128)}, f32[6]{0:T(128)S(1)}, f32[1280,1]{0,1:T(1,128)S(1)}, s32[8]{0:T(128)S(1)}, /*index=5*/s32[1280]{0...) while((s32[]{:T(128)}, f32[8,2,4,540]{3,2,1,0:T(4,128)}, ...), condition=%wide.region_2.3_spmd.clone.clone, body=%wide.region_0.2_spmd.clone.clone.sunk | while | flops 147317040 | bytes 22999700 | solution.py:84
  123.3 0.7 dynamic_slice.39
  124.0 0.7 fusion.46
  124.8 12.4 %fusion.47 = (bf16[1280,1,540]{0,2,1:T(8,128)(2,1)S(1)}, bf16[1280,1,540]{0,2,1:T(8,128)(2,1)S(1)}) fusion(s32[1280]{0:T(1024)S(1)} %get-tuple-element.310, f32[1280]{0:T(1024)S(1)} %get-tuple-element.281, f32[1280]{0:T(1024)S(1)} %get-tuple-element.282, f32[1280]{0:T(1024)S(1)} %reduce.4, f32[1280]{0:T(1024)S(1)} %reduce.5), kind=kLoop, calls=%fused_computation.12.clone.1 | loop fusion | flops 13132800 | bytes 2790400 | tf_op jit(solution)/shard_map/convert
  137.5 7.2 %copy.40 = bf16[1280,2,540]{2,1,0:T(2,128)(2,1)} copy(bf16[1280,2,540]{0,2,1:T(8,128)(2,1)S(1)} %pad_maximum_fusion.4) | data formatting | bytes 5529600 | tf_op jit(solution)/shard_map/while/body/eval_jaxpr/stack | solution.py:74
  144.7 6.6 %convert_element_type.80 = bf16[2560,540]{1,0:T(8,128)(2,1)S(1)} reshape(bf16[1280,2,540]{2,1,0:T(2,128)(2,1)} %copy.40) | data formatting | bytes 5529600 | tf_op jit(solution)/shard_map/while/body/eval_jaxpr/convert_element_type | solution.py:75
  151.3 1.5 convolution_bitcast_fusion.2
  154.3 0.7 fusion.46
  155.1 12.4 %fusion.47 = (bf16[1280,1,540]{0,2,1:T(8,128)(2,1)S(1)}, bf16[1280,1,540]{0,2,1:T(8,128)(2,1)S(1)}) fusion(s32[1280]{0:T(1024)S(1)} %get-tuple-element.310, f32[1280]{0:T(1024)S(1)} %get-tuple-element.281, f32[1280]{0:T(1024)S(1)} %get-tuple-element.282, f32[1280]{0:T(1024)S(1)} %reduce.4, f32[1280]{0:T(1024)S(1)} %reduce.5), kind=kLoop, calls=%fused_computation.12.clone.1 | loop fusion | flops 13132800 | bytes 2790400 | tf_op jit(solution)/shard_map/convert
  167.8 7.2 %copy.40 = bf16[1280,2,540]{2,1,0:T(2,128)(2,1)} copy(bf16[1280,2,540]{0,2,1:T(8,128)(2,1)S(1)} %pad_maximum_fusion.4) | data formatting | bytes 5529600 | tf_op jit(solution)/shard_map/while/body/eval_jaxpr/stack | solution.py:74
  175.0 6.6 %convert_element_type.80 = bf16[2560,540]{1,0:T(8,128)(2,1)S(1)} reshape(bf16[1280,2,540]{2,1,0:T(2,128)(2,1)} %copy.40) | data formatting | bytes 5529600 | tf_op jit(solution)/shard_map/while/body/eval_jaxpr/convert_element_type | solution.py:75
  181.6 1.5 convolution_bitcast_fusion.2
  184.0 0.7 dynamic_slice.39
  184.6 0.7 fusion.46
  185.4 12.4 %fusion.47 = (bf16[1280,1,540]{0,2,1:T(8,128)(2,1)S(1)}, bf16[1280,1,540]{0,2,1:T(8,128)(2,1)S(1)}) fusion(s32[1280]{0:T(1024)S(1)} %get-tuple-element.310, f32[1280]{0:T(1024)S(1)} %get-tuple-element.281, f32[1280]{0:T(1024)S(1)} %get-tuple-element.282, f32[1280]{0:T(1024)S(1)} %reduce.4, f32[1280]{0:T(1024)S(1)} %reduce.5), kind=kLoop, calls=%fused_computation.12.clone.1 | loop fusion | flops 13132800 | bytes 2790400 | tf_op jit(solution)/shard_map/convert
  198.1 7.2 %copy.40 = bf16[1280,2,540]{2,1,0:T(2,128)(2,1)} copy(bf16[1280,2,540]{0,2,1:T(8,128)(2,1)S(1)} %pad_maximum_fusion.4) | data formatting | bytes 5529600 | tf_op jit(solution)/shard_map/while/body/eval_jaxpr/stack | solution.py:74
  205.3 6.6 %convert_element_type.80 = bf16[2560,540]{1,0:T(8,128)(2,1)S(1)} reshape(bf16[1280,2,540]{2,1,0:T(2,128)(2,1)} %copy.40) | data formatting | bytes 5529600 | tf_op jit(solution)/shard_map/while/body/eval_jaxpr/convert_element_type | solution.py:75
  212.0 1.5 convolution_bitcast_fusion.2
  214.9 0.7 fusion.46
  215.7 12.4 %fusion.47 = (bf16[1280,1,540]{0,2,1:T(8,128)(2,1)S(1)}, bf16[1280,1,540]{0,2,1:T(8,128)(2,1)S(1)}) fusion(s32[1280]{0:T(1024)S(1)} %get-tuple-element.310, f32[1280]{0:T(1024)S(1)} %get-tuple-element.281, f32[1280]{0:T(1024)S(1)} %get-tuple-element.282, f32[1280]{0:T(1024)S(1)} %reduce.4, f32[1280]{0:T(1024)S(1)} %reduce.5), kind=kLoop, calls=%fused_computation.12.clone.1 | loop fusion | flops 13132800 | bytes 2790400 | tf_op jit(solution)/shard_map/convert
  228.4 7.2 %copy.40 = bf16[1280,2,540]{2,1,0:T(2,128)(2,1)} copy(bf16[1280,2,540]{0,2,1:T(8,128)(2,1)S(1)} %pad_maximum_fusion.4) | data formatting | bytes 5529600 | tf_op jit(solution)/shard_map/while/body/eval_jaxpr/stack | solution.py:74
  235.6 6.6 %convert_element_type.80 = bf16[2560,540]{1,0:T(8,128)(2,1)S(1)} reshape(bf16[1280,2,540]{2,1,0:T(2,128)(2,1)} %copy.40) | data formatting | bytes 5529600 | tf_op jit(solution)/shard_map/while/body/eval_jaxpr/convert_element_type | solution.py:75
  242.3 1.5 convolution_bitcast_fusion.2
  244.6 0.7 dynamic_slice.39
  245.2 0.7 fusion.46
  246.0 12.4 %fusion.47 = (bf16[1280,1,540]{0,2,1:T(8,128)(2,1)S(1)}, bf16[1280,1,540]{0,2,1:T(8,128)(2,1)S(1)}) fusion(s32[1280]{0:T(1024)S(1)} %get-tuple-element.310, f32[1280]{0:T(1024)S(1)} %get-tuple-element.281, f32[1280]{0:T(1024)S(1)} %get-tuple-element.282, f32[1280]{0:T(1024)S(1)} %reduce.4, f32[1280]{0:T(1024)S(1)} %reduce.5), kind=kLoop, calls=%fused_computation.12.clone.1 | loop fusion | flops 13132800 | bytes 2790400 | tf_op jit(solution)/shard_map/convert
  258.7 7.2 %copy.40 = bf16[1280,2,540]{2,1,0:T(2,128)(2,1)} copy(bf16[1280,2,540]{0,2,1:T(8,128)(2,1)S(1)} %pad_maximum_fusion.4) | data formatting | bytes 5529600 | tf_op jit(solution)/shard_map/while/body/eval_jaxpr/stack | solution.py:74
  266.0 6.6 %convert_element_type.80 = bf16[2560,540]{1,0:T(8,128)(2,1)S(1)} reshape(bf16[1280,2,540]{2,1,0:T(2,128)(2,1)} %copy.40) | data formatting | bytes 5529600 | tf_op jit(solution)/shard_map/while/body/eval_jaxpr/convert_element_type | solution.py:75
  272.6 1.5 convolution_bitcast_fusion.2
  275.6 0.7 fusion.46
  276.4 12.4 %fusion.47 = (bf16[1280,1,540]{0,2,1:T(8,128)(2,1)S(1)}, bf16[1280,1,540]{0,2,1:T(8,128)(2,1)S(1)}) fusion(s32[1280]{0:T(1024)S(1)} %get-tuple-element.310, f32[1280]{0:T(1024)S(1)} %get-tuple-element.281, f32[1280]{0:T(1024)S(1)} %get-tuple-element.282, f32[1280]{0:T(1024)S(1)} %reduce.4, f32[1280]{0:T(1024)S(1)} %reduce.5), kind=kLoop, calls=%fused_computation.12.clone.1 | loop fusion | flops 13132800 | bytes 2790400 | tf_op jit(solution)/shard_map/convert
  289.0 7.2 %copy.40 = bf16[1280,2,540]{2,1,0:T(2,128)(2,1)} copy(bf16[1280,2,540]{0,2,1:T(8,128)(2,1)S(1)} %pad_maximum_fusion.4) | data formatting | bytes 5529600 | tf_op jit(solution)/shard_map/while/body/eval_jaxpr/stack | solution.py:74
  296.3 6.6 %convert_element_type.80 = bf16[2560,540]{1,0:T(8,128)(2,1)S(1)} reshape(bf16[1280,2,540]{2,1,0:T(2,128)(2,1)} %copy.40) | data formatting | bytes 5529600 | tf_op jit(solution)/shard_map/while/body/eval_jaxpr/convert_element_type | solution.py:75
  302.9 1.5 convolution_bitcast_fusion.2
  305.9 0.7 fusion.46
  306.7 12.4 %fusion.47 = (bf16[1280,1,540]{0,2,1:T(8,128)(2,1)S(1)}, bf16[1280,1,540]{0,2,1:T(8,128)(2,1)S(1)}) fusion(s32[1280]{0:T(1024)S(1)} %get-tuple-element.310, f32[1280]{0:T(1024)S(1)} %get-tuple-element.281, f32[1280]{0:T(1024)S(1)} %get-tuple-element.282, f32[1280]{0:T(1024)S(1)} %reduce.4, f32[1280]{0:T(1024)S(1)} %reduce.5), kind=kLoop, calls=%fused_computation.12.clone.1 | loop fusion | flops 13132800 | bytes 2790400 | tf_op jit(solution)/shard_map/convert
  319.3 7.2 %copy.40 = bf16[1280,2,540]{2,1,0:T(2,128)(2,1)} copy(bf16[1280,2,540]{0,2,1:T(8,128)(2,1)S(1)} %pad_maximum_fusion.4) | data formatting | bytes 5529600 | tf_op jit(solution)/shard_map/while/body/eval_jaxpr/stack | solution.py:74
  326.6 6.6 %convert_element_type.80 = bf16[2560,540]{1,0:T(8,128)(2,1)S(1)} reshape(bf16[1280,2,540]{2,1,0:T(2,128)(2,1)} %copy.40) | data formatting | bytes 5529600 | tf_op jit(solution)/shard_map/while/body/eval_jaxpr/convert_element_type | solution.py:75
  333.2 1.5 convolution_bitcast_fusion.2
  336.2 0.7 fusion.46
  337.0 12.4 %fusion.47 = (bf16[1280,1,540]{0,2,1:T(8,128)(2,1)S(1)}, bf16[1280,1,540]{0,2,1:T(8,128)(2,1)S(1)}) fusion(s32[1280]{0:T(1024)S(1)} %get-tuple-element.310, f32[1280]{0:T(1024)S(1)} %get-tuple-element.281, f32[1280]{0:T(1024)S(1)} %get-tuple-element.282, f32[1280]{0:T(1024)S(1)} %reduce.4, f32[1280]{0:T(1024)S(1)} %reduce.5), kind=kLoop, calls=%fused_computation.12.clone.1 | loop fusion | flops 13132800 | bytes 2790400 | tf_op jit(solution)/shard_map/convert
  349.6 7.2 %copy.40 = bf16[1280,2,540]{2,1,0:T(2,128)(2,1)} copy(bf16[1280,2,540]{0,2,1:T(8,128)(2,1)S(1)} %pad_maximum_fusion.4) | data formatting | bytes 5529600 | tf_op jit(solution)/shard_map/while/body/eval_jaxpr/stack | solution.py:74
  356.9 6.6 %convert_element_type.80 = bf16[2560,540]{1,0:T(8,128)(2,1)S(1)} reshape(bf16[1280,2,540]{2,1,0:T(2,128)(2,1)} %copy.40) | data formatting | bytes 5529600 | tf_op jit(solution)/shard_map/while/body/eval_jaxpr/convert_element_type | solution.py:75
  363.5 1.5 convolution_bitcast_fusion.2
  365.8 0.9 copy.29
  366.8 0.8 reshape.277
  367.7 35.3 %all-reduce.2.cloned.1.call-done = f32[2,4,4320]{2,1,0:T(4,128)} async-done(((f32[2,4,4320]{2,1,0:T(4,128)}), f32[2,4,4320]{2,1,0:T(4,128)}) %all-reduce.2.cloned.1.call-update) | async-done | bytes 138256 | tf_op jit(solution)/shard_map/psum | solution.py:90
  403.1 1.0 constant_dynamic-update-slice_fusion.7
  404.1 4.2 collective-permute-done
  408.3 1.0 pad_maximum_fusion.2
  409.8 4.0 collective-permute-done.1
  413.8 1.0 pad_maximum_fusion.1
  414.8 1.2 collective-permute-start.2
  416.0 14.0 %collective-permute-done.2 = f32[8,4,4320]{2,1,0:T(4,128)S(1)} collective-permute-done((f32[8,4,4320]{2,1,0:T(4,128)S(1)}, f32[8,4,4320]{2,1,0:T(4,128)S(1)}, u32[]{:S(2)}, u32[]{:S(2)}) %collective-permute-start.2) | collective-permute-done | bytes 552992 | tf_op jit(solution)/shard_map/ppermute | solution.py:101
  431.9 0.7 fusion.34
  (99 shorter events, 15.6 us)
Async XLA Ops:
  60.9 52.4 %copy-start.1 = (s32[1280]{0:T(1024)S(1)}, s32[1280]{0:T(1024)}, u32[]{:S(2)}) copy-start(s32[1280]{0:T(1024)} %param.12) | copy-start | bytes 15364
  60.9 52.4 %copy-start.3 = (s32[16]{0:T(128)S(1)}, s32[16]{0:T(128)}, u32[]{:S(2)}) copy-start(s32[16]{0:T(128)} %param.14) | copy-start | bytes 196
  109.0 10.6 %all-to-all-start = ((bf16[320,8,48]{0,2,1:T(8,128)(2,1)}), bf16[320,8,48]{0,2,1:T(8,128)(2,1)S(1)}, u32[]{:S(2)}, u32[]{:S(2)}) async-start(bf16[320,8,48]{0,2,1:T(8,128)(2,1)} %copy.25), calls=%async_computation | async-start | bytes 589824 | tf_op jit(solution)/shard_map/all_to_all | solution.py:52
  113.3 289.8 %all-reduce.2.cloned.1.call-start = ((), (), s32[]{:S(2)}) async-start(), calls=%async_computation.1 | async-start | bytes 278528 | tf_op jit(solution)/shard_map/psum | solution.py:90
  113.3 10.0 %copy-start.2 = (f32[6]{0:T(128)S(1)}, f32[6]{0:T(128)}, u32[]{:S(2)}) copy-start(f32[6]{0:T(128)} %param.13) | copy-start | bytes 76
  123.3 244.3 %copy-start.4 = (f32[16]{0:T(128)S(1)}, f32[16]{0:T(128)}, u32[]{:S(2)}) copy-start(f32[16]{0:T(128)} %param.15) | copy-start | bytes 196
  403.1 27.1 %copy-start = (f32[2,4,4320]{2,1,0:T(4,128)S(1)}, f32[2,4,4320]{2,1,0:T(4,128)}, u32[]{:S(2)}) copy-start(f32[2,4,4320]{2,1,0:T(4,128)} %all-reduce.2.cloned.1.call-done) | copy-start | bytes 414724
  403.1 5.3 %collective-permute-start = (f32[2,4,4320]{2,1,0:T(4,128)}, f32[2,4,4320]{2,1,0:T(4,128)S(1)}, u32[]{:S(2)}, u32[]{:S(2)}) collective-permute-start(f32[2,4,4320]{2,1,0:T(4,128)} %all-reduce.2.cloned.1.call-done), channel_id=1, source_target_pairs={{0,25},{1,0},{8,1},{9,8},{16,9},{17,16},{24,17},{25,24},{2,27},{3,... | collective-permute-start | bytes 414728 | tf_op jit(solution)/shard_map/ppermute | solution.py:101
  409.3 4.5 %collective-permute-start.1 = (f32[4,4,4320]{2,1,0:T(4,128)S(1)}, f32[4,4,4320]{2,1,0:T(4,128)S(1)}, u32[]{:S(2)}, u32[]{:S(2)}) collective-permute-start(f32[4,4,4320]{2,1,0:T(4,128)S(1)} %pad_maximum_fusion.2), channel_id=1, source_target_pairs={{0,24},{1,25},{8,0},{9,1},{16,8},{17,9},{24,16},{25,17},{2,26},{3,... | collective-permute-start | bytes 829448 | tf_op jit(solution)/shard_map/ppermute | solution.py:101
  414.8 15.2 %collective-permute-start.2 = (f32[8,4,4320]{2,1,0:T(4,128)S(1)}, f32[8,4,4320]{2,1,0:T(4,128)S(1)}, u32[]{:S(2)}, u32[]{:S(2)}) collective-permute-start(f32[8,4,4320]{2,1,0:T(4,128)S(1)} %pad_maximum_fusion.1), channel_id=1, source_target_pairs={{0,16},{1,17},{8,24},{9,25},{16,0},{17,1},{24,8},{25,9},{2,18},{3,... | collective-permute-start | bytes 1658888 | tf_op jit(solution)/shard_map/ppermute | solution.py:101
Sparse Core Ops, SparseCore 0:
  367.7 35.2 all-reduce.1
